TPU v7x, 128 devices: a whole 4x4x4 slice. The times are simulated.
128 devices in a mesh: ep: 32 (over z, x, core), tp: 4 (over y).
Axes of the slice: x: 4, y: 4, z: 4, core: 2. Of those that a mesh axis runs over, the one named last changes fastest.
Arguments:
- stream: bfloat16 [16384, 2048], P('ep'), may hold values from -6 to 6
- queries: bfloat16 [16384, 2048], P('ep', 'tp'), may hold values from -6 to 6
- keys_in: bfloat16 [16384, 2048], P('ep', 'tp'), may hold values from -6 to 6
- values_in: bfloat16 [16384, 2048], P('ep', 'tp'), may hold values from -6 to 6
- segment_ids: int32 [32, 512], P('ep'), may hold values from 0 to 5, never falling along the last dimension, each value on 1 to 256 neighbouring positions
- routes: int32 [16384, 4], P('ep'), may hold values from 0 to 63, all different within a row; in each aligned block of 512 rows (0 to 511, 512 to 1023, ...) at most 48 rows name the same one
- route_weights: float32 [16384, 4], P('ep'), may hold values from 0.1 to 0.6
- w_out: bfloat16 [2048, 2048], P('tp'), may hold values from -0.125 to 0.125
- norm_gain: float32 [2048], replicated, may hold values from 0.25 to 1.75
- expert_gate: bfloat16 [64, 2048, 1408], P('ep', None, 'tp'), may hold values from -0.125 to 0.125
- expert_up: bfloat16 [64, 2048, 1408], P('ep', None, 'tp'), may hold values from -0.125 to 0.125
- expert_down: bfloat16 [64, 1408, 2048], P('ep', 'tp'), may hold values from -0.15625 to 0.15625
- shared_gate: bfloat16 [2048, 3584], P(None, 'tp'), may hold values from -0.125 to 0.125
- shared_up: bfloat16 [2048, 3584], P(None, 'tp'), may hold values from -0.125 to 0.125
- shared_down: bfloat16 [3584, 2048], P('tp'), may hold values from -0.09375 to 0.09375
- shared_router: bfloat16 [2048], replicated, may hold values from -0.125 to 0.125
Outputs:
- mixed: bfloat16 [16384, 2048], P('ep', 'tp')
Inputs may be any that keep to these rules, and one draw needn't show every extreme that they name: `routes`: in each aligned block of 512 rows, no expert is named by more than 48 rows, a bound that some block reaches. `segment_ids`: segment numbers never fall within a block; each prompt has at most 256 tokens, and some has exactly 256.
All inputs are finite; a program needn't handle non-finite values.
Results may differ from a plain program's by a relative error of at most 0.012.
Values may be sent and summed in bfloat16 or wider, within the bound.
No kernel may reach another device: no remote copies, remote signals or barrier semaphores. Data moves between devices by JAX's collectives and lax.ppermute only.
A program may use at most 128 MiB of HBM per device.

v0:
```python
import jax
import jax.numpy as jnp
from jax import lax
from jax.sharding import PartitionSpec as P

HEAD = 128


def slots_of(block_routes, experts, capacity):
    length, picks = block_routes.shape
    flat = block_routes.reshape(length * picks)
    onehot = (flat[:, None] == jnp.arange(experts, dtype=jnp.int32)[None, :]).astype(jnp.int32)
    before = jnp.cumsum(onehot, axis=0, dtype=jnp.int32) - onehot
    rank = jnp.sum(before * onehot, axis=1, dtype=jnp.int32)
    slot = flat * capacity + rank
    owners = jnp.arange(length * picks, dtype=jnp.int32) // picks
    table = jnp.full((experts * capacity,), -1, dtype=jnp.int32).at[slot].set(owners)
    return (slot.reshape(length, picks), table)


def attend_local(query_block, key_block, value_block, segment):
    length = query_block.shape[0]
    heads = query_block.shape[1] // HEAD
    places = jnp.arange(length, dtype=jnp.int32)
    allowed = (segment[:, None] == segment[None, :]) & (places[:, None] >= places[None, :])

    def one_head(operands):
        query_rows, key_rows, value_rows = operands
        scores = jnp.dot(query_rows, key_rows.T, preferred_element_type=jnp.float32) * HEAD ** (
            -0.5
        )
        scores = jnp.where(allowed, scores, -jnp.inf)
        highest = jnp.max(scores, axis=1, keepdims=True)
        weights = jnp.exp(scores - highest)
        shares = (weights / jnp.sum(weights, axis=1, keepdims=True)).astype(jnp.bfloat16)
        return jnp.dot(shares, value_rows, preferred_element_type=jnp.float32).astype(jnp.bfloat16)

    def by_head(values):
        return values.reshape(length, heads, HEAD).transpose(1, 0, 2)

    attended = lax.map(one_head, (by_head(query_block), by_head(key_block), by_head(value_block)))
    return attended.transpose(1, 0, 2).reshape(length, heads * HEAD)


def on_device(
    stream,
    queries,
    keys_in,
    values_in,
    segment_ids,
    routes,
    route_weights,
    w_out,
    norm_gain,
    expert_gate,
    expert_up,
    expert_down,
    shared_gate,
    shared_up,
    shared_down,
    shared_router,
):
    length, width = stream.shape
    ep_count = lax.axis_size("ep")
    tp_count = lax.axis_size("tp")
    attended = attend_local(queries, keys_in, values_in, segment_ids[0])
    partial_value = jnp.dot(attended, w_out, preferred_element_type=jnp.float32)
    resid = stream.astype(jnp.float32) + lax.psum(partial_value.astype(jnp.bfloat16), "tp").astype(
        jnp.float32
    )
    normed = (
        resid * lax.rsqrt(jnp.mean(resid * resid, axis=1, keepdims=True) + 1e-06) * norm_gain
    ).astype(jnp.bfloat16)
    shared_gate_rows = jnp.dot(normed, shared_gate, preferred_element_type=jnp.float32)
    shared_up_rows = jnp.dot(normed, shared_up, preferred_element_type=jnp.float32)
    shared_hidden = (jax.nn.silu(shared_gate_rows) * shared_up_rows).astype(jnp.bfloat16)
    shared_part = jnp.dot(shared_hidden, shared_down, preferred_element_type=jnp.float32)
    shared_cols = lax.psum_scatter(
        shared_part.astype(jnp.bfloat16), "tp", scatter_dimension=1, tiled=True
    ).astype(jnp.float32)
    shared_scale = jax.nn.sigmoid(
        jnp.dot(normed, shared_router, preferred_element_type=jnp.float32)
    )
    local_experts = expert_gate.shape[0]
    experts = local_experts * ep_count
    picks = routes.shape[1]
    divisor = 2 * experts * tp_count
    capacity = tp_count * ((3 * length * picks + divisor - 1) // divisor)
    slot, table = slots_of(routes, experts, capacity)
    live = table >= 0
    outgoing = jnp.take(normed, jnp.maximum(table, 0), axis=0)
    outgoing = jnp.where(live[:, None], outgoing, jnp.zeros_like(outgoing))
    outgoing = outgoing.reshape(ep_count, local_experts, capacity, width)
    incoming = lax.all_to_all(outgoing, "ep", split_axis=0, concat_axis=0, tiled=True)
    gate_rows = jnp.einsum(
        "sjcd,jdf->sjcf", incoming, expert_gate, preferred_element_type=jnp.float32
    )
    up_rows = jnp.einsum("sjcd,jdf->sjcf", incoming, expert_up, preferred_element_type=jnp.float32)
    expert_hidden = (jax.nn.silu(gate_rows) * up_rows).astype(jnp.bfloat16)
    expert_part = jnp.einsum(
        "sjcf,jfd->sjcd", expert_hidden, expert_down, preferred_element_type=jnp.float32
    )
    expert_cols = lax.psum_scatter(
        expert_part.astype(jnp.bfloat16), "tp", scatter_dimension=3, tiled=True
    )
    returned = lax.all_to_all(expert_cols, "ep", split_axis=0, concat_axis=0, tiled=True)
    columns = returned.shape[3]
    flat_results = returned.reshape(experts * capacity, columns)
    picked = (
        jnp.take(flat_results, slot.reshape(-1), axis=0)
        .reshape(length, picks, columns)
        .astype(jnp.float32)
    )
    routed = jnp.sum(picked * route_weights[:, :, None], axis=1)
    resid_cols = lax.dynamic_slice_in_dim(resid, lax.axis_index("tp") * columns, columns, 1)
    return (resid_cols + shared_scale[:, None] * shared_cols + routed).astype(jnp.bfloat16)


def solution(mesh):
    placed = (
        P("ep", None),
        P("ep", "tp"),
        P("ep", "tp"),
        P("ep", "tp"),
        P("ep", None),
        P("ep", None),
        P("ep", None),
        P("tp", None),
        P(),
        P("ep", None, "tp"),
        P("ep", None, "tp"),
        P("ep", "tp", None),
        P(None, "tp"),
        P(None, "tp"),
        P("tp", None),
        P(),
    )
    return jax.shard_map(
        on_device, mesh=mesh, in_specs=placed, out_specs=P("ep", "tp"), check_vma=False
    )
```

profile of v0, /device:TPU:0, one launch (start us, length us, event | category | flops | bytes accessed | tf_op | source)
XLA Modules:
  0.0 510.2 jit_solution(16891996998942227729)
XLA Ops:
  6.5 2.2 copy.52
  8.7 2.1 copy.53
  10.8 2.1 copy.54
  12.9 14.5 %while.11 = (s32[]{:T(128)}, bf16[4,512,128]{1,2,0:T(8,128)(2,1)}, bf16[4,512,128]{1,2,0:T(8,128)(2,1)}, bf16[4,512,128]{1,2,0:T(8,128)(2,1)}, bf16[4,512,128]{1,2,0:T(8,128)(2,1)}, /*index=5*/s32[512]{0:T(512)}, s32[]{:T(128)}) while((s32[]{:T(128)}, bf16[4,512,128]{1,2,0:T(8,128)(2,1)}, bf16[4,512,128]{1,2,0:T(8,128)(2,1)}, ...), condition=%wide.region_3.4_spmd.clone, body=%wide.region_0.3_spmd.clone.sunk | while | flops 137165824 | bytes 4209757 | solution.py:41
  12.9 1.3 fusion.63
  14.2 0.2 fusion.64
  14.4 1.3 fusion.65
  15.7 0.1 copy.90
  15.8 0.7 constant_dynamic-update-slice_fusion.2
  16.5 1.3 fusion.63
  17.8 0.2 fusion.64
  18.0 1.3 fusion.65
  19.3 0.1 copy.90
  19.4 0.7 constant_dynamic-update-slice_fusion.2
  20.1 1.3 fusion.63
  21.5 0.2 fusion.64
  21.7 1.3 fusion.65
  22.9 0.1 copy.90
  23.1 0.7 constant_dynamic-update-slice_fusion.2
  23.7 1.3 fusion.63
  25.1 0.2 fusion.64
  25.3 1.3 fusion.65
  26.6 0.1 copy.90
  26.7 0.7 constant_dynamic-update-slice_fusion.2
  27.4 4.3 convolution_convert_fusion.2
  31.8 0.1 copy.59
  31.9 0.2 eq.45
  32.1 0.2 reshape.113
  32.3 0.1 copy.65
  32.4 0.2 mul.90
  32.6 0.8 fusion.38
  33.5 31.5 %reduce-window.6 = s32[64,16,128]{2,1,0:T(8,128)S(1)} reduce-window(s32[64,16,128]{2,1,0:T(8,128)} %fusion.38, s32[]{:T(128)} %constant.82.clone.1), window={size=1x1x128 pad=0_0x0_0x127_0}, to_apply=%region_7.8 | reduce-window | flops 16646144 | bytes 1048580 | tf_op jit(solution)/shard_map/reduce-window
  65.0 1.0 slice.12
  66.0 1.5 copy.73
  67.5 0.2 reduce-window.9
  67.7 0.2 broadcast_add_fusion
  67.9 0.3 fusion.37
  68.1 8.1 %scatter_custom_fusion = s32[3072]{0:T(1024)S(1)} fusion(s32[2048]{0:T(1024)S(1)} %bitcast.120, s32[2048]{0:T(1024)S(1)} %add_select_fusion, s32[]{:T(128)} %constant.94.clone.1), kind=kCustom, calls=%fused_computation.68 | custom fusion | bytes 12292 | tf_op jit(solution)/shard_map/scatter | solution.py:17
  76.3 0.1 broadcast_in_dim.67
  76.4 16.7 %all-reduce.2.cloned.1.call-done = bf16[512,2048]{1,0:T(8,128)(2,1)} async-done(((bf16[512,2048]{1,0:T(8,128)(2,1)}), bf16[512,2048]{1,0:T(8,128)(2,1)}) %all-reduce.2.cloned.1.call-update) | async-done | bytes 2097168 | tf_op jit(solution)/shard_map/psum | solution.py:68
  93.1 5.0 convert_add_fusion
  98.2 2.3 multiply_convert_fusion
  100.5 25.7 %gather_fusion = bf16[3072,2048]{1,0:T(8,128)(2,1)} fusion(bf16[512,2048]{1,0:T(8,128)(2,1)} %multiply_convert_fusion, s32[3072]{0:T(1024)S(1)} %maximum_clamp_fusion), kind=kCustom, calls=%fused_computation | custom fusion | bytes 25178112 | tf_op jit(solution)/shard_map/jit(_take)/gather | solution.py:91
  126.2 7.0 %select_select_fusion = bf16[32,2,48,2048]{3,2,1,0:T(8,128)(2,1)S(1)} fusion(bf16[32,2,48,2048]{3,2,1,0:T(8,128)(2,1)} %bitcast.114, pred[32,2,48]{2,1,0:T(4,128)(4,1)S(1)} %broadcast_in_dim.67, pred[32,2,48]{2,1,0:T(4,128)(4,1)S(1)} %broadcast_in_dim.65), kind=kLoop, calls=%fused_computation.23 | loop fusion | flops 12582912 | bytes 25171968 | tf_op jit(solution)/shard_map/jit(_where)/select_n | solution.py:92
  133.2 148.1 %all_to_all.10 = bf16[32,2,48,2048]{3,2,1,0:T(8,128)(2,1)S(1)} all-to-all(bf16[32,2,48,2048]{3,2,1,0:T(8,128)(2,1)S(1)} %select_select_fusion), channel_id=1, replica_groups=mesh['ep'=32,'tp'=4] {'ep'}, dimensions={0} | all-to-all | bytes 25165824 | tf_op jit(solution)/shard_map/all_to_all | solution.py:94
  281.3 4.5 copy-done.1
  285.7 8.6 %fusion.14 = f32[2,32,48,352]{3,2,1,0:T(8,128)} fusion(bf16[32,2,48,2048]{3,2,1,0:T(8,128)(2,1)S(1)} %all_to_all.10, bf16[2,2048,352]{1,2,0:T(8,128)(2,1)S(1)} %copy-done.8), kind=kOutput, calls=%fused_computation.24 | convolution fusion | flops 4429185024 | bytes 19791872 | tf_op jit(solution)/shard_map/sjcd,jdf->sjcf/dot_general | solution.py:98
  294.3 20.3 %convert_bitcast_fusion = bf16[32,2,48,2048]{3,2,0,1:T(8,128)(2,1)} fusion(bf16[2,352,2048]{2,1,0:T(8,128)(2,1)S(1)} %copy-done, f32[2,32,48,352]{3,2,1,0:T(8,128)} %fusion.14, bf16[32,2,48,2048]{3,2,1,0:T(8,128)(2,1)} %copy-done.1, bf16[2,2048,352]{1,2,0:T(8,128)(2,1)} %param.27), kind=kOutput, calls=%fused_computation.22 | convolution fusion | flops 8871149568 | bytes 35258368 | tf_op jit(solution)/shard_map/sjcf,jfd->sjcd/dot_general | solution.py:100
  314.7 0.3 reduce-scatter.3.cloned.1.call-start
  314.9 6.3 %fusion.48 = f32[512,896]{1,0:T(8,128)} fusion(bf16[512,2048]{1,0:T(8,128)(2,1)} %multiply_convert_fusion, bf16[2048,896]{1,0:T(8,128)(2,1)} %param.30), kind=kOutput, calls=%fused_computation.78 | convolution fusion | flops 1879048192 | bytes 7602176 | tf_op jit(solution)/shard_map/dot_general | solution.py:74
  321.2 10.2 %convolution_convert_fusion.1 = bf16[512,2048]{1,0:T(8,128)(2,1)} fusion(bf16[896,2048]{1,0:T(8,128)(2,1)} %param.32, f32[512,896]{1,0:T(8,128)} %fusion.48, bf16[512,2048]{1,0:T(8,128)(2,1)} %multiply_convert_fusion, bf16[2048,896]{1,0:T(8,128)(2,1)} %param.31), kind=kOutput, calls=%fused_computation.39 | convolution fusion | flops 3761897472 | bytes 13369344 | tf_op jit(solution)/shard_map/dot_general | solution.py:77
  331.4 94.2 %reduce-scatter.5.cloned.1.call-done = bf16[32,2,48,512]{3,2,0,1:T(8,128)(2,1)} async-done(((bf16[32,2,48,2048]{3,2,0,1:T(8,128)(2,1)}), bf16[32,2,48,512]{3,2,0,1:T(8,128)(2,1)}) %reduce-scatter.5.cloned.1.call-update) | async-done | bytes 3145744 | tf_op jit(solution)/shard_map/reduce_scatter | solution.py:103
  425.6 3.9 copy.68
  429.5 7.5 %all-to-all-start.1 = ((bf16[32,2,48,512]{3,2,1,0:T(8,128)(2,1)}), bf16[32,2,48,512]{3,2,1,0:T(8,128)(2,1)}, u32[]{:S(2)}, u32[]{:S(2)}) async-start(bf16[32,2,48,512]{3,2,1,0:T(8,128)(2,1)} %copy.68), calls=%async_computation.3 | async-start | bytes 6291456 | tf_op jit(solution)/shard_map/all_to_all | solution.py:106
  437.0 0.3 reduce_sum.42
  437.3 0.1 copy.69
  437.4 0.1 copy.63
  437.6 0.2 copy.64
  437.8 2.2 fusion.47
  440.0 38.9 %all-to-all-done.1 = bf16[32,2,48,512]{3,2,1,0:T(8,128)(2,1)} async-done(((bf16[32,2,48,512]{3,2,1,0:T(8,128)(2,1)}), bf16[32,2,48,512]{3,2,1,0:T(8,128)(2,1)}, u32[]{:S(2)}, u32[]{:S(2)}) %all-to-all-start.1) | async-done | bytes 3145760 | tf_op jit(solution)/shard_map/all_to_all | solution.py:106
  479.0 11.5 %gather_fusion.1 = bf16[2048,512]{1,0:T(8,128)(2,1)} fusion(bf16[3072,512]{1,0:T(8,128)(2,1)} %bitcast.25, s32[2048]{0:T(1024)S(1)} %broadcast_clamp_fusion), kind=kCustom, calls=%fused_computation.1 | custom fusion | bytes 4202496 | tf_op jit(solution)/shard_map/jit(_take)/gather | solution.py:110
  490.5 4.0 gather.15
  494.5 6.5 %multiply_reduce_fusion = f32[512,512]{1,0:T(8,128)} fusion(f32[512,4]{1,0:T(8,128)S(1)} %copy.69, bf16[512,4,512]{2,1,0:T(4,128)(2,1)} %gather.15, pred[512,4]{1,0:T(8,128)(4,1)S(1)} %copy.64), kind=kLoop, calls=%fused_computation.35 | loop fusion | flops 3932160 | bytes 3155968 | tf_op jit(solution)/shard_map/reduce_sum | solution.py:114
  501.0 2.7 add_convert_fusion
  (35 shorter events, 0.3 us)
Async XLA Ops:
  6.5 287.8 %copy-start = (bf16[2,352,2048]{2,1,0:T(8,128)(2,1)S(1)}, bf16[2,352,2048]{2,1,0:T(8,128)(2,1)}, u32[]{:S(2)}) copy-start(bf16[2,352,2048]{2,1,0:T(8,128)(2,1)} %param.29) | copy-start | bytes 8650756
  6.5 86.6 %all-reduce.2.cloned.1.call-start = ((), (), s32[]{:S(2)}) async-start(), calls=%async_computation.4 | async-start | bytes 4194304 | tf_op jit(solution)/shard_map/psum | solution.py:68
  27.4 4.4 copy-start.4
  31.7 393.9 %reduce-scatter.5.cloned.1.call-start = ((), (), s32[]{:S(2)}) async-start(), calls=%async_computation.6 | async-start | bytes 15728640 | tf_op jit(solution)/shard_map/reduce_scatter | solution.py:103
  76.4 21.7 %copy-start.5 = (f32[2048]{0:T(1024)S(1)}, f32[2048]{0:T(1024)}, u32[]{:S(2)}) copy-start(f32[2048]{0:T(1024)} %param.26) | copy-start | bytes 24580
  93.1 5.0 copy-start.2
  93.1 5.0 copy-start.3
  133.1 152.6 %copy-start.8 = (bf16[2,2048,352]{1,2,0:T(8,128)(2,1)S(1)}, bf16[2,2048,352]{1,2,0:T(8,128)(2,1)}, u32[]{:S(2)}) copy-start(bf16[2,2048,352]{1,2,0:T(8,128)(2,1)} %param.28) | copy-start | bytes 8650756
  281.2 4.5 copy-start.1
  314.7 186.3 %reduce-scatter.3.cloned.1.call-start = ((), (), s32[]{:S(2)}) async-start(), calls=%async_computation.5 | async-start | bytes 2621440 | tf_op jit(solution)/shard_map/reduce_scatter | solution.py:78
  429.5 7.8 %copy-start.7 = (bf16[2048]{0:T(1024)(128)(2,1)S(1)}, bf16[2048]{0:T(1024)(128)(2,1)}, u32[]{:S(2)}) copy-start(bf16[2048]{0:T(1024)(128)(2,1)} %param.33) | copy-start | bytes 12292
  429.5 7.8 %copy-start.6 = (f32[512,4]{0,1:T(4,128)S(1)}, f32[512,4]{0,1:T(4,128)}, u32[]{:S(2)}) copy-start(f32[512,4]{0,1:T(4,128)} %param.24) | copy-start | bytes 24580
  429.5 49.5 %all-to-all-start.1 = ((bf16[32,2,48,512]{3,2,1,0:T(8,128)(2,1)}), bf16[32,2,48,512]{3,2,1,0:T(8,128)(2,1)}, u32[]{:S(2)}, u32[]{:S(2)}) async-start(bf16[32,2,48,512]{3,2,1,0:T(8,128)(2,1)} %copy.68), calls=%async_computation.3 | async-start | bytes 6291456 | tf_op jit(solution)/shard_map/all_to_all | solution.py:106
Sparse Core Ops, SparseCore 0:
  31.9 61.2 all-reduce.1
  314.8 110.7 reduce-scatter.4
  428.0 29.4 reduce-scatter.2
where the time goes:
time: 513 us; the launch traced here: 510 us
  waiting for transfers between devices  150 us (29%)
  blocking collectives  148 us (29%)
  local copies, waits for them, and re-layouts  71.3 us (14%)
  matrix products  62.4 us (12%)
  other arithmetic  57.4 us (11%)
  between operations  13.3 us (3%)
  starting transfers between devices  7.79 us (2%)
    all_to_all x1, blocking collectives, on_device(): lax.all_to_all(outgoing, 'ep', split_axis=0, concat_axis=0, tiled=True)  148 us
    reduce_scatter x1, waiting for transfers between devices, on_device(): lax.psum_scatter(expert_part.astype(jnp.bfloat16), 'tp', scatter_dimensio...  94.2 us
    all_to_all x1, waiting for transfers between devices, on_device(): lax.all_to_all(expert_cols, 'ep', split_axis=0, concat_axis=0, tiled=True)  38.9 us
    another operation x3, other arithmetic  31.9 us
    gather x1, local copies, waits for them, and re-layouts, on_device(): outgoing = jnp.take(normed, jnp.maximum(table, 0), axis=0)  25.7 us
    dot_general x1, matrix products, on_device(): jnp.einsum('sjcf,jfd->sjcd', expert_hidden, expert_down, preferred_elemen...  20.3 us
    psum x1, waiting for transfers between devices, on_device(): lax.psum(partial_value.astype(jnp.bfloat16), 'tp').astype(jnp.float32)  16.7 us
    gather x2, local copies, waits for them, and re-layouts, on_device(): jnp.take(flat_results, slot.reshape(-1), axis=0)  15.5 us
  transfers between devices with their start and end apart: 4, of which 3 were waited for; matrix products, arithmetic and copies ran while one was open for 18% of the time, Pallas kernels for 0%

commit v1 on v0

--- a/solution.py
+++ b/solution.py
@@ -65,9 +65,9 @@
     tp_count = lax.axis_size("tp")
     attended = attend_local(queries, keys_in, values_in, segment_ids[0])
     partial_value = jnp.dot(attended, w_out, preferred_element_type=jnp.float32)
-    resid = stream.astype(jnp.float32) + lax.psum(partial_value.astype(jnp.bfloat16), "tp").astype(
-        jnp.float32
-    )
+    resid = stream.astype(jnp.float32) + jnp.sum(
+        lax.all_gather(partial_value.astype(jnp.bfloat16), "tp"), axis=0
+    ).astype(jnp.float32)
     normed = (
         resid * lax.rsqrt(jnp.mean(resid * resid, axis=1, keepdims=True) + 1e-06) * norm_gain
     ).astype(jnp.bfloat16)

time: 513 us -> 546 us (1.064)
  waiting for transfers between devices: 150 us -> 175 us
  other arithmetic: 57.4 us -> 64.7 us
    all_gather x0 -> x1, waiting for transfers between devices: none -> 41 us  [on_device(): lax.all_gather(partial_value.astype(jnp.bfloat16), 'tp')]
    psum x1 -> x0, waiting for transfers between devices: 16.7 us -> none  [on_device(): lax.psum(partial_value.astype(jnp.bfloat16), 'tp').astype(jnp.float32)]
    reduce_sum x0 -> x1, other arithmetic: none -> 7.27 us  [on_device(): jnp.sum(lax.all_gather(partial_value.astype(jnp.bfloat16), 'tp'), axis=0)]
  transfers between devices with their start and end apart: 4 -> 4, of which waited for: 3 -> 3; matrix products, arithmetic and copies ran while one was open for 18% -> 17% of each run, Pallas kernels for 0% -> 0%
where the time goes in v1:
time: 546 us; the launch traced here: 543 us
  waiting for transfers between devices  175 us (32%)
  blocking collectives  148 us (27%)
  local copies, waits for them, and re-layouts  71.2 us (13%)
  other arithmetic  64.7 us (12%)
  matrix products  63 us (12%)
  between operations  13.3 us (2%)
  starting transfers between devices  7.8 us (1%)
    all_to_all x1, blocking collectives, on_device(): lax.all_to_all(outgoing, 'ep', split_axis=0, concat_axis=0, tiled=True)  148 us
    reduce_scatter x1, waiting for transfers between devices, on_device(): lax.psum_scatter(expert_part.astype(jnp.bfloat16), 'tp', scatter_dimensio...  94.9 us
    all_gather x1, waiting for transfers between devices, on_device(): lax.all_gather(partial_value.astype(jnp.bfloat16), 'tp')  41 us
    all_to_all x1, waiting for transfers between devices, on_device(): lax.all_to_all(expert_cols, 'ep', split_axis=0, concat_axis=0, tiled=True)  38.9 us
    another operation x3, other arithmetic  32 us
    gather x1, local copies, waits for them, and re-layouts, on_device(): outgoing = jnp.take(normed, jnp.maximum(table, 0), axis=0)  25.7 us
    dot_general x1, matrix products, on_device(): jnp.einsum('sjcf,jfd->sjcd', expert_hidden, expert_down, preferred_elemen...  20.3 us
    gather x2, local copies, waits for them, and re-layouts, on_device(): jnp.take(flat_results, slot.reshape(-1), axis=0)  15.5 us
  transfers between devices with their start and end apart: 4, of which 3 were waited for; matrix products, arithmetic and copies ran while one was open for 17% of the time, Pallas kernels for 0%

profile of v1, /device:TPU:0, one launch (start us, length us, event | category | flops | bytes accessed | tf_op | source)
XLA Modules:
  0.0 543.2 jit_solution(6399092690206121977)
XLA Ops:
  6.5 2.2 copy.52
  8.7 2.1 copy.53
  10.8 2.1 copy.54
  12.9 14.5 %while.11 = (s32[]{:T(128)}, bf16[4,512,128]{1,2,0:T(8,128)(2,1)}, bf16[4,512,128]{1,2,0:T(8,128)(2,1)}, bf16[4,512,128]{1,2,0:T(8,128)(2,1)}, bf16[4,512,128]{1,2,0:T(8,128)(2,1)}, /*index=5*/s32[512]{0:T(512)}, s32[]{:T(128)}) while((s32[]{:T(128)}, bf16[4,512,128]{1,2,0:T(8,128)(2,1)}, bf16[4,512,128]{1,2,0:T(8,128)(2,1)}, ...), condition=%wide.region_3.4_spmd.clone, body=%wide.region_0.3_spmd.clone.sunk | while | flops 137165824 | bytes 4209757 | solution.py:41
  12.9 1.3 fusion.63
  14.2 0.2 fusion.64
  14.4 1.3 fusion.65
  15.7 0.1 copy.91
  15.8 0.7 constant_dynamic-update-slice_fusion.2
  16.5 1.3 fusion.63
  17.8 0.2 fusion.64
  18.0 1.3 fusion.65
  19.3 0.1 copy.91
  19.4 0.7 constant_dynamic-update-slice_fusion.2
  20.1 1.3 fusion.63
  21.5 0.2 fusion.64
  21.7 1.3 fusion.65
  22.9 0.1 copy.91
  23.1 0.7 constant_dynamic-update-slice_fusion.2
  23.7 1.3 fusion.63
  25.1 0.2 fusion.64
  25.3 1.3 fusion.65
  26.6 0.1 copy.91
  26.7 0.7 constant_dynamic-update-slice_fusion.2
  27.4 4.4 convolution_convert_fusion.2
  31.9 0.1 copy.59
  32.0 0.2 eq.45
  32.2 0.2 reshape.113
  32.4 0.1 copy.65
  32.5 0.2 mul.90
  32.7 0.8 fusion.38
  33.6 31.6 %reduce-window.6 = s32[64,16,128]{2,1,0:T(8,128)S(1)} reduce-window(s32[64,16,128]{2,1,0:T(8,128)} %fusion.38, s32[]{:T(128)} %constant.83.clone.1), window={size=1x1x128 pad=0_0x0_0x127_0}, to_apply=%region_7.8 | reduce-window | flops 16646144 | bytes 1048580 | tf_op jit(solution)/shard_map/reduce-window
  65.1 1.0 slice.12
  66.1 1.5 copy.73
  67.6 0.2 reduce-window.9
  67.8 0.2 broadcast_add_fusion
  68.0 0.3 fusion.37
  68.3 8.1 %scatter_custom_fusion = s32[3072]{0:T(1024)S(1)} fusion(s32[2048]{0:T(1024)S(1)} %bitcast.122, s32[2048]{0:T(1024)S(1)} %add_select_fusion, s32[]{:T(128)} %constant.95.clone.1), kind=kCustom, calls=%fused_computation.68 | custom fusion | bytes 12292 | tf_op jit(solution)/shard_map/scatter | solution.py:17
  76.6 41.0 %all-gather.3.cloned.1.call-done = bf16[2048,2048]{1,0:T(8,128)(2,1)} async-done(((bf16[512,2048]{1,0:T(8,128)(2,1)}), bf16[2048,2048]{1,0:T(8,128)(2,1)}) %all-gather.3.cloned.1.call-update) | async-done | bytes 8388624 | tf_op jit(solution)/shard_map/all_gather | solution.py:69
  117.6 7.3 %reduce_sum.52 = bf16[512,2048]{1,0:T(8,128)(2,1)} reduce(bf16[4,512,2048]{2,1,0:T(8,128)(2,1)} %bitcast.116, bf16[]{:T(256)} %constant.84.clone.1), dimensions={0}, to_apply=%region_4.5 | reduce | flops 3145728 | bytes 10485762 | tf_op jit(solution)/shard_map/reduce_sum | solution.py:68
  124.8 5.0 convert_add_fusion
  129.9 2.3 multiply_convert_fusion
  132.2 25.7 %gather_fusion = bf16[3072,2048]{1,0:T(8,128)(2,1)} fusion(bf16[512,2048]{1,0:T(8,128)(2,1)} %multiply_convert_fusion, s32[3072]{0:T(1024)S(1)} %maximum_clamp_fusion), kind=kCustom, calls=%fused_computation | custom fusion | bytes 25178112 | tf_op jit(solution)/shard_map/jit(_take)/gather | solution.py:91
  157.9 7.0 %select_select_fusion = bf16[32,2,48,2048]{3,2,1,0:T(8,128)(2,1)S(1)} fusion(bf16[32,2,48,2048]{3,2,1,0:T(8,128)(2,1)} %bitcast.115, pred[32,2,48]{2,1,0:T(4,128)(4,1)S(1)} %broadcast_in_dim.67, pred[32,2,48]{2,1,0:T(4,128)(4,1)S(1)} %broadcast_in_dim.65), kind=kLoop, calls=%fused_computation.23 | loop fusion | flops 12582912 | bytes 25171968 | tf_op jit(solution)/shard_map/jit(_where)/select_n | solution.py:92
  164.9 148.2 %all_to_all.10 = bf16[32,2,48,2048]{3,2,1,0:T(8,128)(2,1)S(1)} all-to-all(bf16[32,2,48,2048]{3,2,1,0:T(8,128)(2,1)S(1)} %select_select_fusion), channel_id=1, replica_groups=mesh['ep'=32,'tp'=4] {'ep'}, dimensions={0} | all-to-all | bytes 25165824 | tf_op jit(solution)/shard_map/all_to_all | solution.py:94
  313.0 4.5 copy-done.2
  317.5 8.6 %fusion.14 = f32[2,32,48,352]{3,2,1,0:T(8,128)} fusion(bf16[32,2,48,2048]{3,2,1,0:T(8,128)(2,1)S(1)} %all_to_all.10, bf16[2,2048,352]{1,2,0:T(8,128)(2,1)S(1)} %copy-done.8), kind=kOutput, calls=%fused_computation.24 | convolution fusion | flops 4429185024 | bytes 19791872 | tf_op jit(solution)/shard_map/sjcd,jdf->sjcf/dot_general | solution.py:98
  326.1 20.3 %convert_bitcast_fusion = bf16[32,2,48,2048]{3,2,0,1:T(8,128)(2,1)} fusion(bf16[2,352,2048]{2,1,0:T(8,128)(2,1)S(1)} %copy-done, f32[2,32,48,352]{3,2,1,0:T(8,128)} %fusion.14, bf16[32,2,48,2048]{3,2,1,0:T(8,128)(2,1)} %copy-done.2, bf16[2,2048,352]{1,2,0:T(8,128)(2,1)} %param.27), kind=kOutput, calls=%fused_computation.22 | convolution fusion | flops 8871149568 | bytes 35258368 | tf_op jit(solution)/shard_map/sjcf,jfd->sjcd/dot_general | solution.py:100
  346.5 0.3 reduce-scatter.3.cloned.1.call-start
  346.7 6.3 %fusion.48 = f32[512,896]{1,0:T(8,128)} fusion(bf16[512,2048]{1,0:T(8,128)(2,1)} %multiply_convert_fusion, bf16[2048,896]{1,0:T(8,128)(2,1)} %param.30), kind=kOutput, calls=%fused_computation.78 | convolution fusion | flops 1879048192 | bytes 7602176 | tf_op jit(solution)/shard_map/dot_general | solution.py:74
  353.0 10.6 %convolution_convert_fusion.1 = bf16[512,2048]{1,0:T(8,128)(2,1)} fusion(bf16[896,2048]{1,0:T(8,128)(2,1)} %param.32, f32[512,896]{1,0:T(8,128)} %fusion.48, bf16[512,2048]{1,0:T(8,128)(2,1)} %multiply_convert_fusion, bf16[2048,896]{1,0:T(8,128)(2,1)} %param.31), kind=kOutput, calls=%fused_computation.39 | convolution fusion | flops 3761897472 | bytes 13369344 | tf_op jit(solution)/shard_map/dot_general | solution.py:77
  363.6 94.9 %reduce-scatter.5.cloned.1.call-done = bf16[32,2,48,512]{3,2,0,1:T(8,128)(2,1)} async-done(((bf16[32,2,48,2048]{3,2,0,1:T(8,128)(2,1)}), bf16[32,2,48,512]{3,2,0,1:T(8,128)(2,1)}) %reduce-scatter.5.cloned.1.call-update) | async-done | bytes 3145744 | tf_op jit(solution)/shard_map/reduce_scatter | solution.py:103
  458.5 3.9 copy.68
  462.4 7.5 %all-to-all-start.1 = ((bf16[32,2,48,512]{3,2,1,0:T(8,128)(2,1)}), bf16[32,2,48,512]{3,2,1,0:T(8,128)(2,1)}, u32[]{:S(2)}, u32[]{:S(2)}) async-start(bf16[32,2,48,512]{3,2,1,0:T(8,128)(2,1)} %copy.68), calls=%async_computation.3 | async-start | bytes 6291456 | tf_op jit(solution)/shard_map/all_to_all | solution.py:106
  469.9 0.3 reduce_sum.55
  470.2 0.1 copy.69
  470.4 0.1 copy.63
  470.5 0.2 copy.64
  470.7 2.2 fusion.47
  473.0 38.9 %all-to-all-done.1 = bf16[32,2,48,512]{3,2,1,0:T(8,128)(2,1)} async-done(((bf16[32,2,48,512]{3,2,1,0:T(8,128)(2,1)}), bf16[32,2,48,512]{3,2,1,0:T(8,128)(2,1)}, u32[]{:S(2)}, u32[]{:S(2)}) %all-to-all-start.1) | async-done | bytes 3145760 | tf_op jit(solution)/shard_map/all_to_all | solution.py:106
  511.9 11.5 %gather_fusion.1 = bf16[2048,512]{1,0:T(8,128)(2,1)} fusion(bf16[3072,512]{1,0:T(8,128)(2,1)} %bitcast.26, s32[2048]{0:T(1024)S(1)} %broadcast_clamp_fusion), kind=kCustom, calls=%fused_computation.1 | custom fusion | bytes 4202496 | tf_op jit(solution)/shard_map/jit(_take)/gather | solution.py:110
  523.4 4.0 gather.15
  527.4 6.5 %multiply_reduce_fusion = f32[512,512]{1,0:T(8,128)} fusion(f32[512,4]{1,0:T(8,128)S(1)} %copy.69, bf16[512,4,512]{2,1,0:T(4,128)(2,1)} %gather.15, pred[512,4]{1,0:T(8,128)(4,1)S(1)} %copy.64), kind=kLoop, calls=%fused_computation.35 | loop fusion | flops 3932160 | bytes 3155968 | tf_op jit(solution)/shard_map/reduce_sum | solution.py:114
  533.9 2.7 add_convert_fusion
  (36 shorter events, 0.4 us)
Async XLA Ops:
  6.5 319.6 %copy-start = (bf16[2,352,2048]{2,1,0:T(8,128)(2,1)S(1)}, bf16[2,352,2048]{2,1,0:T(8,128)(2,1)}, u32[]{:S(2)}) copy-start(bf16[2,352,2048]{2,1,0:T(8,128)(2,1)} %param.29) | copy-start | bytes 8650756
  6.5 111.0 %all-gather.3.cloned.1.call-start = ((), (), s32[]{:S(2)}) async-start(), calls=%async_computation.6 | async-start | bytes 10485760 | tf_op jit(solution)/shard_map/all_gather | solution.py:69
  27.4 4.5 copy-start.4
  31.8 426.7 %reduce-scatter.5.cloned.1.call-start = ((), (), s32[]{:S(2)}) async-start(), calls=%async_computation.5 | async-start | bytes 15728640 | tf_op jit(solution)/shard_map/reduce_scatter | solution.py:103
  124.8 5.0 copy-start.1
  124.8 5.0 copy-start.3
  124.8 5.0 copy-start.5
  164.9 152.7 %copy-start.8 = (bf16[2,2048,352]{1,2,0:T(8,128)(2,1)S(1)}, bf16[2,2048,352]{1,2,0:T(8,128)(2,1)}, u32[]{:S(2)}) copy-start(bf16[2,2048,352]{1,2,0:T(8,128)(2,1)} %param.28) | copy-start | bytes 8650756
  313.0 4.5 copy-start.2
  346.5 187.4 %reduce-scatter.3.cloned.1.call-start = ((), (), s32[]{:S(2)}) async-start(), calls=%async_computation.4 | async-start | bytes 2621440 | tf_op jit(solution)/shard_map/reduce_scatter | solution.py:78
  462.4 7.8 %copy-start.7 = (bf16[2048]{0:T(1024)(128)(2,1)S(1)}, bf16[2048]{0:T(1024)(128)(2,1)}, u32[]{:S(2)}) copy-start(bf16[2048]{0:T(1024)(128)(2,1)} %param.33) | copy-start | bytes 12292
  462.4 7.8 %copy-start.6 = (f32[512,4]{0,1:T(4,128)S(1)}, f32[512,4]{0,1:T(4,128)}, u32[]{:S(2)}) copy-start(f32[512,4]{0,1:T(4,128)} %param.24) | copy-start | bytes 24580
  462.4 49.5 %all-to-all-start.1 = ((bf16[32,2,48,512]{3,2,1,0:T(8,128)(2,1)}), bf16[32,2,48,512]{3,2,1,0:T(8,128)(2,1)}, u32[]{:S(2)}, u32[]{:S(2)}) async-start(bf16[32,2,48,512]{3,2,1,0:T(8,128)(2,1)} %copy.68), calls=%async_computation.3 | async-start | bytes 6291456 | tf_op jit(solution)/shard_map/all_to_all | solution.py:106
Sparse Core Ops, SparseCore 0:
  32.0 85.5 all-gather.2
  346.6 111.9 reduce-scatter.4
  460.9 29.4 reduce-scatter.2
